TPU v7x, 32 devices: a whole 2x2x4 slice. The times are simulated.
32 devices in a mesh: mem: 8 (over z, y), head: 4 (over x, core).
Axes of the slice: x: 2, y: 2, z: 4, core: 2. Of those that a mesh axis runs over, the one named last changes fastest.
Arguments:
- queries: bfloat16 [4096, 2048], P('mem', 'head'), may hold values from -8 to 8
- local_keys: bfloat16 [4096, 2048], P('mem', 'head'), may hold values from -8 to 8
- local_values: bfloat16 [4096, 2048], P('mem', 'head'), may hold values from -8 to 8
- memory_keys: bfloat16 [128, 32, 2048], P('mem', None, 'head'), may hold values from -8 to 8
- memory_values: bfloat16 [128, 32, 2048], P('mem', None, 'head'), may hold values from -8 to 8
- retrieval: int32 [8, 32], replicated, may hold values from 0 to 127, as said below
- gate_logit: float32 [16], P('head'), may hold values from -4 to 4
- dropout_keep: int32 [4096, 2048], P('mem', 'head'), may hold values 0 or 1
- out_weight: bfloat16 [2048, 2048], P('head'), may hold values from -0.125 to 0.125
- cotangent: bfloat16 [4096, 2048], P('mem', 'head'), may hold values from -6 to 6
Outputs:
- layer_out: bfloat16 [4096, 2048], P('mem', 'head')
- grad_queries: bfloat16 [4096, 2048], P('mem', 'head')
- grad_keys: bfloat16 [4096, 2048], P('mem', 'head')
- grad_values: bfloat16 [4096, 2048], P('mem', 'head')
- grad_memory_keys: bfloat16 [128, 32, 2048], P('mem', None, 'head')
- grad_memory_values: bfloat16 [128, 32, 2048], P('mem', None, 'head')
Inputs may be any that keep to these rules, and one draw needn't show every extreme that they name: `retrieval`: block i lies on shard i // 16. Rows d * 1 to (d + 1) - 1 belong to index d of mem; together they name 32 distinct blocks, at most 8 of them on any one shard, and in every draw one shard receives exactly 8 from the rows of every index.
All inputs are finite; a program needn't handle non-finite values. No bound on the sum of `dropout_keep` on one device may be relied on, other than what follows from the above.
Results may differ from a plain program's by a relative error of at most 0.0079.
Values may be sent and summed in bfloat16 or wider, within the bound.
No kernel may reach another device: no remote copies, remote signals or barrier semaphores. Data moves between devices by JAX's collectives and lax.ppermute only.
A program may use at most 128 MiB of HBM per device.

v0:
```python
import jax
import jax.numpy as jnp
from jax import lax
from jax.sharding import PartitionSpec as P

QBLK = 512
keep_scale = 1.0 / 0.9


def contract_last(left, right):
    return lax.dot_general(
        left, right, (((1,), (1,)), ((), ())), preferred_element_type=jnp.float32
    )


def contract_first(left, right):
    return lax.dot_general(
        left, right, (((0,), (0,)), ((), ())), preferred_element_type=jnp.float32
    )


def branch_weights(query_rows, keyset, causal):
    score_scale = query_rows.shape[1] ** (-0.5)
    scores = contract_last(query_rows, keyset) * score_scale
    if causal:
        row_iota = lax.broadcasted_iota(jnp.int32, scores.shape, 0)
        col_iota = lax.broadcasted_iota(jnp.int32, scores.shape, 1)
        scores = jnp.where(col_iota <= row_iota, scores, -jnp.inf)
    return jnp.exp(scores - jnp.max(scores, axis=1, keepdims=True))


def branch_forward(query_rows, keyset, valueset, causal):
    weights = branch_weights(query_rows, keyset, causal)
    row_total = jnp.sum(weights, axis=1, keepdims=True)
    mixed_out = (
        jnp.dot(weights.astype(jnp.bfloat16), valueset, preferred_element_type=jnp.float32)
        / row_total
    )
    return (mixed_out, row_total)


def branch_backward(query_rows, keyset, valueset, row_total, mixed_out, grad_mixed, causal):
    weights = branch_weights(query_rows, keyset, causal)
    probabilities = weights / row_total
    delta_rows = jnp.sum(grad_mixed * mixed_out, axis=1, keepdims=True)
    grad_low = grad_mixed.astype(jnp.bfloat16)
    grad_probs = contract_last(grad_low, valueset)
    score_scale = query_rows.shape[1] ** (-0.5)
    grad_scores = (probabilities * (grad_probs - delta_rows) * score_scale).astype(jnp.bfloat16)
    grad_query = jnp.dot(grad_scores, keyset, preferred_element_type=jnp.float32)
    grad_keyset = contract_first(grad_scores, query_rows)
    grad_valueset = contract_first(probabilities.astype(jnp.bfloat16), grad_low)
    return (grad_query, grad_keyset, grad_valueset)


def per_device(
    queries,
    local_keys,
    local_values,
    memory_keys,
    memory_values,
    retrieval,
    gate_logit,
    dropout_keep,
    out_weight,
    cotangent,
):
    mem_count = lax.axis_size("mem")
    mem_index = lax.axis_index("mem")
    tok_rows, feature_cols = queries.shape
    heads_here = gate_logit.shape[0]
    head_dim = feature_cols // heads_here
    blocks_here = memory_keys.shape[0]
    block_len = memory_keys.shape[1]
    query_blocks = tok_rows // QBLK
    top_blocks = retrieval.shape[1]
    request_count = query_blocks * top_blocks
    capacity = 2 * request_count // mem_count
    slot_count = mem_count * capacity
    entries = block_len * feature_cols
    owner_ids = retrieval // blocks_here
    local_ids = retrieval % blocks_here
    earlier_mask = lax.broadcasted_iota(
        jnp.int32, (request_count, request_count), 0
    ) < lax.broadcasted_iota(jnp.int32, (request_count, request_count), 1)
    same_owner = owner_ids[:, :, None] == owner_ids[:, None, :]
    owner_rank = jnp.sum((same_owner & earlier_mask[None]).astype(jnp.int32), axis=1)
    request_owner = lax.dynamic_index_in_dim(owner_ids, mem_index, 0, keepdims=False)
    request_rank = lax.dynamic_index_in_dim(owner_rank, mem_index, 0, keepdims=False)
    request_slot = request_owner * capacity + request_rank
    slot_iota = lax.broadcasted_iota(jnp.int32, (request_count, slot_count), 1)
    pick_table = (request_slot[:, None] == slot_iota).astype(jnp.bfloat16)
    cap_iota = lax.broadcasted_iota(jnp.int32, (mem_count, request_count, capacity), 2)
    wanted = (owner_ids[:, :, None] == mem_index) & (owner_rank[:, :, None] == cap_iota)
    send_local = jnp.sum(wanted.astype(jnp.int32) * (local_ids[:, :, None] + 1), axis=1) - 1
    block_iota = lax.broadcasted_iota(jnp.int32, (slot_count, blocks_here), 1)
    serve_table = (send_local.reshape(slot_count, 1) == block_iota).astype(jnp.bfloat16)

    def outgoing(table):
        flat_rows = table.reshape(blocks_here, entries)
        served = jnp.dot(serve_table, flat_rows, preferred_element_type=jnp.float32)
        return served.astype(jnp.bfloat16).reshape(mem_count, capacity, block_len, feature_cols)

    def selected(blocks):
        flat_rows = blocks.reshape(slot_count, entries)
        chosen = jnp.dot(pick_table, flat_rows, preferred_element_type=jnp.float32)
        return chosen.astype(jnp.bfloat16).reshape(top_blocks * block_len, feature_cols)

    fetched = (
        lax.all_to_all(outgoing(memory_keys), "mem", split_axis=0, concat_axis=0, tiled=True),
        lax.all_to_all(outgoing(memory_values), "mem", split_axis=0, concat_axis=0, tiled=True),
    )
    gate_values = 1.0 / (1.0 + jnp.exp(-gate_logit))
    keep_mask = dropout_keep.astype(jnp.float32)
    saved_state = []
    block_index = 0
    row_start = block_index * QBLK
    row_stop = row_start + QBLK
    mem_keyset = selected(fetched[0])
    mem_valueset = selected(fetched[1])
    head_parts = []
    for head_index in range(heads_here):
        col_start = head_index * head_dim
        col_stop = col_start + head_dim
        query_rows = queries[row_start:row_stop, col_start:col_stop]
        mixed_loc, total_loc = branch_forward(
            query_rows,
            local_keys[row_start:row_stop, col_start:col_stop],
            local_values[row_start:row_stop, col_start:col_stop],
            True,
        )
        mixed_mem, total_mem = branch_forward(
            query_rows,
            mem_keyset[:, col_start:col_stop],
            mem_valueset[:, col_start:col_stop],
            False,
        )
        saved_state.append((mixed_loc, total_loc, mixed_mem, total_mem))
        head_parts.append(
            gate_values[head_index] * mixed_mem + (1.0 - gate_values[head_index]) * mixed_loc
        )
    attended_parts = jnp.concatenate(head_parts, axis=1)
    dropped = (attended_parts * keep_mask * keep_scale).astype(jnp.bfloat16)
    partial_out = jnp.dot(dropped, out_weight, preferred_element_type=jnp.float32)
    layer_out = lax.psum_scatter(partial_out, "head", scatter_dimension=1, tiled=True).astype(
        jnp.bfloat16
    )
    cotangent_full = lax.all_gather(cotangent, "head", axis=1, tiled=True)
    grad_attended = contract_last(cotangent_full, out_weight) * keep_mask * keep_scale
    query_grads, key_grads, value_grads, memkey_parts, memvalue_parts = ([], [], [], [], [])
    block_index = 0
    row_start = block_index * QBLK
    row_stop = row_start + QBLK
    mem_keyset = selected(fetched[0])
    mem_valueset = selected(fetched[1])
    head_query = []
    head_key = []
    head_value = []
    head_memkey = []
    head_memvalue = []
    for head_index in range(heads_here):
        col_start = head_index * head_dim
        col_stop = col_start + head_dim
        mixed_loc, total_loc, mixed_mem, total_mem = saved_state[
            block_index * heads_here + head_index
        ]
        query_rows = queries[row_start:row_stop, col_start:col_stop]
        grad_here = grad_attended[row_start:row_stop, col_start:col_stop]
        query_mem, keyset_mem, valueset_mem = branch_backward(
            query_rows,
            mem_keyset[:, col_start:col_stop],
            mem_valueset[:, col_start:col_stop],
            total_mem,
            mixed_mem,
            gate_values[head_index] * grad_here,
            False,
        )
        query_loc, keyset_loc, valueset_loc = branch_backward(
            query_rows,
            local_keys[row_start:row_stop, col_start:col_stop],
            local_values[row_start:row_stop, col_start:col_stop],
            total_loc,
            mixed_loc,
            (1.0 - gate_values[head_index]) * grad_here,
            True,
        )
        head_query.append((query_mem + query_loc).astype(jnp.bfloat16))
        head_key.append(keyset_loc.astype(jnp.bfloat16))
        head_value.append(valueset_loc.astype(jnp.bfloat16))
        head_memkey.append(keyset_mem.astype(jnp.bfloat16))
        head_memvalue.append(valueset_mem.astype(jnp.bfloat16))
    query_grads.append(jnp.concatenate(head_query, axis=1))
    key_grads.append(jnp.concatenate(head_key, axis=1))
    value_grads.append(jnp.concatenate(head_value, axis=1))
    memkey_parts.append(jnp.concatenate(head_memkey, axis=1).reshape(top_blocks, entries))
    memvalue_parts.append(jnp.concatenate(head_memvalue, axis=1).reshape(top_blocks, entries))
    send_keys = contract_first(pick_table, memkey_parts[0]).astype(jnp.bfloat16)
    send_values = contract_first(pick_table, memvalue_parts[0]).astype(jnp.bfloat16)
    returned = (
        lax.all_to_all(
            send_keys.reshape(mem_count, capacity, block_len, feature_cols),
            "mem",
            split_axis=0,
            concat_axis=0,
            tiled=True,
        ),
        lax.all_to_all(
            send_values.reshape(mem_count, capacity, block_len, feature_cols),
            "mem",
            split_axis=0,
            concat_axis=0,
            tiled=True,
        ),
    )
    grad_memory_keys = contract_first(serve_table, returned[0].reshape(slot_count, entries)).astype(
        jnp.bfloat16
    )
    grad_memory_values = contract_first(
        serve_table, returned[1].reshape(slot_count, entries)
    ).astype(jnp.bfloat16)
    return (
        layer_out,
        query_grads[0],
        key_grads[0],
        value_grads[0],
        grad_memory_keys.reshape(blocks_here, block_len, feature_cols),
        grad_memory_values.reshape(blocks_here, block_len, feature_cols),
    )


def solution(mesh):
    placed = (
        P("mem", "head"),
        P("mem", "head"),
        P("mem", "head"),
        P("mem", None, "head"),
        P("mem", None, "head"),
        P(),
        P("head"),
        P("mem", "head"),
        P("head", None),
        P("mem", "head"),
    )
    return jax.shard_map(
        per_device,
        mesh=mesh,
        in_specs=placed,
        out_specs=(
            P("mem", "head"),
            P("mem", "head"),
            P("mem", "head"),
            P("mem", "head"),
            P("mem", None, "head"),
            P("mem", None, "head"),
        ),
        check_vma=False,
    )
```

profile of v0, /device:TPU:0, one launch (start us, length us, event | category | flops | bytes accessed | tf_op | source)
XLA Modules:
  0.0 273.9 jit_solution(1934526136832263948)
XLA Ops:
  9.2 1.3 copy.64
  10.5 2.1 convolution_convert_fusion.3
  12.6 7.4 %all-to-all-start = ((bf16[8,8,32,512]{3,1,2,0:T(8,128)(2,1)}), bf16[8,8,32,512]{3,1,2,0:T(8,128)(2,1)}, u32[]{:S(2)}, u32[]{:S(2)}) async-start(bf16[8,8,32,512]{3,1,2,0:T(8,128)(2,1)} %bitcast.85), calls=%async_computation | async-start | bytes 4194304 | tf_op jit(solution)/shard_map/all_to_all | solution.py:110
  20.7 1.3 copy.65
  22.8 1.2 fusion.196
  25.2 1.3 fusion.193
  26.5 1.3 fusion.194
  27.8 2.1 convolution_convert_fusion.2
  29.9 38.5 %all-to-all-done = bf16[8,8,32,512]{3,1,2,0:T(8,128)(2,1)} async-done(((bf16[8,8,32,512]{3,1,2,0:T(8,128)(2,1)}), bf16[8,8,32,512]{3,1,2,0:T(8,128)(2,1)}, u32[]{:S(2)}, u32[]{:S(2)}) %all-to-all-start) | async-done | bytes 2097184 | tf_op jit(solution)/shard_map/all_to_all | solution.py:110
  68.4 4.3 %all-to-all-start.1 = ((bf16[8,8,32,512]{3,1,2,0:T(8,128)(2,1)}), bf16[8,8,32,512]{3,1,2,0:T(8,128)(2,1)}, u32[]{:S(2)}, u32[]{:S(2)}) async-start(bf16[8,8,32,512]{3,1,2,0:T(8,128)(2,1)} %bitcast.84), calls=%async_computation.1 | async-start | bytes 4194304 | tf_op jit(solution)/shard_map/all_to_all | solution.py:111
  75.2 2.5 copy.42
  77.7 1.5 fusion.56
  79.3 1.4 fusion.65
  80.7 1.3 fusion.195
  84.3 1.0 convolution_divide_fusion.1
  85.4 3.0 %fusion.8 = f32[512,512]{0,1:T(8,128)S(1)} fusion(bf16[512,2048]{1,0:T(8,128)(2,1)} %all-gather.2.cloned.1.call-done, bf16[512,2048]{1,0:T(8,128)(2,1)S(1)} %copy-done, s32[512,512]{0,1:T(8,128)S(1)} %copy-done.21), kind=kOutput, calls=%fused_computation.37 | convolution fusion | flops 1074528256 | bytes 6291456 | tf_op jit(solution)/shard_map/dot_general | solution.py:11
  89.4 3.1 %convolution_convert_fusion.5 = bf16[32,16384]{1,0:T(8,128)(2,1)} fusion(bf16[64,16384]{1,0:T(8,128)(2,1)} %bitcast.3, s32[32]{0:T(128)S(1)} %add_bitcast_fusion), kind=kOutput, calls=%fused_computation.5 | convolution fusion | flops 67635200 | bytes 3145856 | tf_op jit(solution)/shard_map/dot_general | solution.py:106
  92.4 1.6 reshape.126
  94.0 2.7 multiply_reduce_fusion
  96.7 1.8 multiply_reduce_fusion.1
  98.6 1.8 multiply_reduce_fusion.2
  100.3 1.7 multiply_reduce_fusion.3
  102.1 18.4 %all-to-all-done.1 = bf16[8,8,32,512]{3,1,2,0:T(8,128)(2,1)} async-done(((bf16[8,8,32,512]{3,1,2,0:T(8,128)(2,1)}), bf16[8,8,32,512]{3,1,2,0:T(8,128)(2,1)}, u32[]{:S(2)}, u32[]{:S(2)}) %all-to-all-start.1) | async-done | bytes 2097184 | tf_op jit(solution)/shard_map/all_to_all | solution.py:111
  120.5 3.1 %convolution_convert_fusion.4 = bf16[32,16384]{1,0:T(8,128)(2,1)} fusion(bf16[64,16384]{1,0:T(8,128)(2,1)} %bitcast.5, s32[32]{0:T(128)S(1)} %add_bitcast_fusion), kind=kOutput, calls=%fused_computation.4 | convolution fusion | flops 67635200 | bytes 3145856 | tf_op jit(solution)/shard_map/dot_general | solution.py:106
  123.6 2.3 reshape.130
  125.9 2.1 fusion.31
  128.2 1.6 convolution_divide_fusion.4
  132.0 3.3 %multiply_reduce_fusion.10 = (f32[512]{0:T(512)}, f32[512]{0:T(512)}, f32[512]{0:T(512)S(1)}, f32[512]{0:T(512)}, f32[512]{0:T(512)S(1)}, /*index=5*/f32[512]{0:...) fusion(f32[512,512]{0,1:T(8,128)S(1)} %copy-done.76, f32[]{:T(128)S(6)} %sub.91, ...), kind=kOutput, calls=%fused_computation.151 | convolution fusion | flops 69268480 | bytes 4342800 | tf_op jit(solution)/shard_map/dot_general | solution.py:36
  135.3 1.3 fusion.3
  136.7 1.4 fusion.1
  138.6 1.2 convolution_convert_fusion.13
  141.0 1.1 copy-done.2
  142.4 1.7 multiply_reduce_fusion.11
  144.2 1.2 fusion.5
  145.5 1.3 fusion.7
  146.8 1.2 convolution_convert_fusion.15
  148.0 1.2 convolution_convert_fusion.14
  149.2 3.4 %fusion.71 = f32[512,2048]{1,0:T(8,128)} fusion(bf16[512,2048]{1,0:T(8,128)(2,1)S(1)} %copy-done, f32[512,128]{0,1:T(8,128)S(1)} %get-tuple-element.35, f32[512,128]{0,1:T(8,128)S(1)} %get-tuple-element.34, f32[512,128]{0,1:T(8,128)S(1)} %get-tuple-element.36, f32[512,128]{0,1:T(8,128)S(1)} %get-tuple-element.37, s32[512,512]{0,1:T(8,128)S(1)} %copy-done.22), kind=kOutput, calls=%fused_computation.132 | convolution fusion | flops 1075576832 | bytes 8388608 | tf_op jit(solution)/shard_map/dot_general | solution.py:144
  155.1 2.2 convolution_convert_fusion.1
  157.3 3.8 %all-to-all-start.2 = ((bf16[8,8,32,512]{3,1,2,0:T(8,128)(2,1)}), bf16[8,8,32,512]{3,1,2,0:T(8,128)(2,1)S(1)}, u32[]{:S(2)}, u32[]{:S(2)}) async-start(bf16[8,8,32,512]{3,1,2,0:T(8,128)(2,1)} %bitcast.83), calls=%async_computation.3 | async-start | bytes 4194304 | tf_op jit(solution)/shard_map/all_to_all | solution.py:200
  161.2 1.8 convolution_convert_fusion.19
  165.8 2.0 copy.55
  167.9 3.3 %convolution_convert_fusion.8 = bf16[1024,128]{0,1:T(8,128)(2,1)S(1)} fusion(f32[1024,512]{1,0:T(8,128)} %get-tuple-element.47, f32[512]{0:T(512)S(1)} %copy-done.68, f32[512]{0:T(512)S(1)} %copy-done.48, f32[512,512]{0,1:T(8,128)} %copy-done.75, f32[]{:T(128)} %bitcast.8), kind=kOutput, calls=%fused_computation.70 | convolution fusion | flops 136577024 | bytes 2626048 | tf_op jit(solution)/shard_map/dot_general | solution.py:17
  171.2 1.4 convolution_convert_fusion.9
  172.8 1.3 convolution_convert_fusion.10
  174.4 1.2 convolution_convert_fusion.11
  175.6 1.0 pad_maximum_fusion.1
  176.7 2.3 copy.52
  179.0 2.3 reshape.135
  181.3 1.8 fusion.36
  183.1 1.4 convolution_convert_fusion.23
  184.6 2.3 fusion.33
  186.8 2.1 convolution_convert_fusion
  189.0 20.5 %all-to-all-done.2 = bf16[8,8,32,512]{3,1,2,0:T(8,128)(2,1)S(1)} async-done(((bf16[8,8,32,512]{3,1,2,0:T(8,128)(2,1)}), bf16[8,8,32,512]{3,1,2,0:T(8,128)(2,1)S(1)}, u32[]{:S(2)}, u32[]{:S(2)}) %all-to-all-start.2) | async-done | bytes 2097184 | tf_op jit(solution)/shard_map/all_to_all | solution.py:200
  209.5 4.5 %all-to-all-start.3 = ((bf16[8,8,32,512]{3,1,2,0:T(8,128)(2,1)}), bf16[8,8,32,512]{3,1,2,0:T(8,128)(2,1)}, u32[]{:S(2)}, u32[]{:S(2)}) async-start(bf16[8,8,32,512]{3,1,2,0:T(8,128)(2,1)} %bitcast.82), calls=%async_computation.4 | async-start | bytes 4194304 | tf_op jit(solution)/shard_map/all_to_all | solution.py:207
  214.0 1.4 convolution_convert_fusion.20
  215.4 1.8 fusion.34
  217.6 1.4 fusion.35
  220.7 2.0 copy.54
  222.7 1.7 fusion.100
  224.4 1.4 fusion.40
  230.7 31.1 %all-to-all-done.3 = bf16[8,8,32,512]{3,1,2,0:T(8,128)(2,1)} async-done(((bf16[8,8,32,512]{3,1,2,0:T(8,128)(2,1)}), bf16[8,8,32,512]{3,1,2,0:T(8,128)(2,1)}, u32[]{:S(2)}, u32[]{:S(2)}) %all-to-all-start.3) | async-done | bytes 2097184 | tf_op jit(solution)/shard_map/all_to_all | solution.py:207
  261.8 2.2 convolution_convert_fusion.6
  265.0 2.1 convert_element_type.216
  (218 shorter events, 25.5 us)
Async XLA Ops:
  7.2 78.2 %copy-start = (bf16[512,2048]{1,0:T(8,128)(2,1)S(1)}, bf16[512,2048]{1,0:T(8,128)(2,1)}, u32[]{:S(2)}) copy-start(bf16[512,2048]{1,0:T(8,128)(2,1)} %param.18) | copy-start | bytes 6291460
  12.6 9.5 %copy-start.74 = (f32[4]{0:T(128)S(1)}, f32[4]{0:T(128)}, u32[]{:S(2)}) copy-start(f32[4]{0:T(128)} %param.16) | copy-start | bytes 52
  12.6 10.2 %copy-start.9 = (bf16[512,512]{1,0:T(8,128)(2,1)S(1)}, bf16[512,512]{1,0:T(8,128)(2,1)}, u32[]{:S(2)}) copy-start(bf16[512,512]{1,0:T(8,128)(2,1)} %param.10) | copy-start | bytes 1572868
  12.6 55.8 %all-to-all-start = ((bf16[8,8,32,512]{3,1,2,0:T(8,128)(2,1)}), bf16[8,8,32,512]{3,1,2,0:T(8,128)(2,1)}, u32[]{:S(2)}, u32[]{:S(2)}) async-start(bf16[8,8,32,512]{3,1,2,0:T(8,128)(2,1)} %bitcast.85), calls=%async_computation | async-start | bytes 4194304 | tf_op jit(solution)/shard_map/all_to_all | solution.py:110
  20.0 65.4 %all-gather.2.cloned.1.call-start = ((), (), s32[]{:S(2)}) async-start(), calls=%async_computation.6 | async-start | bytes 2621440 | tf_op jit(solution)/shard_map/all_gather | solution.py:148
  22.1 3.1 %copy-start.43 = (bf16[512,512]{1,0:T(8,128)(2,1)S(1)}, bf16[512,512]{1,0:T(8,128)(2,1)}, u32[]{:S(2)}) copy-start(bf16[512,512]{1,0:T(8,128)(2,1)} %param.11) | copy-start | bytes 1572868
  24.0 64.3 %copy-start.49 = (f32[512]{0:T(512)}, f32[512]{0:T(512)S(1)}, u32[]{:S(2)}) copy-start(f32[512]{0:T(512)S(1)} %get-tuple-element.52) | copy-start | bytes 6148
  25.2 63.2 %copy-start.51 = (f32[512]{0:T(512)}, f32[512]{0:T(512)S(1)}, u32[]{:S(2)}) copy-start(f32[512]{0:T(512)S(1)} %fusion.59) | copy-start | bytes 6148
  26.5 104.4 %copy-start.55 = (f32[512]{0:T(512)}, f32[512]{0:T(512)S(1)}, u32[]{:S(2)}) copy-start(f32[512]{0:T(512)S(1)} %get-tuple-element.42) | copy-start | bytes 6148
  27.8 55.5 %copy-start.53 = (f32[512]{0:T(512)}, f32[512]{0:T(512)S(1)}, u32[]{:S(2)}) copy-start(f32[512]{0:T(512)S(1)} %get-tuple-element.44) | copy-start | bytes 6148
  68.4 52.2 %all-to-all-start.1 = ((bf16[8,8,32,512]{3,1,2,0:T(8,128)(2,1)}), bf16[8,8,32,512]{3,1,2,0:T(8,128)(2,1)}, u32[]{:S(2)}, u32[]{:S(2)}) async-start(bf16[8,8,32,512]{3,1,2,0:T(8,128)(2,1)} %bitcast.84), calls=%async_computation.1 | async-start | bytes 4194304 | tf_op jit(solution)/shard_map/all_to_all | solution.py:111
  72.7 192.3 %reduce-scatter.2.cloned.1.call-start = ((), (), s32[]{:S(2)}) async-start(), calls=%async_computation.5 | async-start | bytes 5242880 | tf_op jit(solution)/shard_map/reduce_scatter | solution.py:145
  77.7 4.5 %copy-start.30 = (f32[512,512]{0,1:T(8,128)S(1)}, f32[512,512]{0,1:T(8,128)}, u32[]{:S(2)}) copy-start(f32[512,512]{0,1:T(8,128)} %copy-done.29) | copy-start | bytes 3145732
  77.7 4.5 %copy-start.73 = (bf16[512,512]{1,0:T(8,128)(2,1)S(1)}, bf16[512,512]{1,0:T(8,128)(2,1)}, u32[]{:S(2)}) copy-start(bf16[512,512]{1,0:T(8,128)(2,1)} %param.12) | copy-start | bytes 1572868
  79.3 51.6 %copy-start.63 = (f32[512]{0:T(512)}, f32[512]{0:T(512)S(1)}, u32[]{:S(2)}) copy-start(f32[512]{0:T(512)S(1)} %fusion.56) | copy-start | bytes 6148
  80.7 2.6 copy-start.61
  80.7 2.6 copy-start.33
  82.0 2.3 copy-start.37
  82.0 2.3 copy-start.57
  82.2 3.1 %copy-start.59 = (f32[512]{0:T(512)}, f32[512]{0:T(512)S(1)}, u32[]{:S(2)}) copy-start(f32[512]{0:T(512)S(1)} %fusion.62) | copy-start | bytes 6148
  83.3 2.1 copy-start.21
  85.4 3.0 %copy-start.31 = (f32[512,512]{0,1:T(8,128)S(1)}, f32[512,512]{0,1:T(8,128)}, u32[]{:S(2)}) copy-start(f32[512,512]{0,1:T(8,128)} %copy-done.29) | copy-start | bytes 3145732
  94.0 2.7 copy-start.10
  96.7 39.9 %copy-start.47 = (f32[512]{0:T(512)}, f32[512]{0:T(512)S(1)}, u32[]{:S(2)}) copy-start(f32[512]{0:T(512)S(1)} %get-tuple-element.46) | copy-start | bytes 6148
  98.6 36.8 %copy-start.45 = (f32[512]{0:T(512)}, f32[512]{0:T(512)S(1)}, u32[]{:S(2)}) copy-start(f32[512]{0:T(512)S(1)} %get-tuple-element.50) | copy-start | bytes 6148
  125.9 2.2 copy-start.8
  128.2 8.5 %copy-start.67 = (f32[512]{0:T(512)}, f32[512]{0:T(512)S(1)}, u32[]{:S(2)}) copy-start(f32[512]{0:T(512)S(1)} %fusion.31) | copy-start | bytes 6148
  128.2 2.1 copy-start.39
  130.2 5.1 %copy-start.65 = (f32[512]{0:T(512)}, f32[512]{0:T(512)S(1)}, u32[]{:S(2)}) copy-start(f32[512]{0:T(512)S(1)} %fusion.28) | copy-start | bytes 6148
  136.6 1.9 copy-start.13
  138.1 2.0 copy-start.4
  140.4 3.8 %copy-start.71 = (f32[512]{0:T(512)}, f32[512]{0:T(512)S(1)}, u32[]{:S(2)}) copy-start(f32[512]{0:T(512)S(1)} %fusion.25) | copy-start | bytes 6148
  142.4 3.0 %copy-start.69 = (f32[512]{0:T(512)}, f32[512]{0:T(512)S(1)}, u32[]{:S(2)}) copy-start(f32[512]{0:T(512)S(1)} %fusion.22) | copy-start | bytes 6148
  145.4 2.6 copy-start.18
  146.8 2.4 copy-start.16
  146.8 2.4 copy-start.22
  157.3 3.8 %copy-start.56 = (f32[512]{0:T(512)S(1)}, f32[512]{0:T(512)}, u32[]{:S(2)}) copy-start(f32[512]{0:T(512)} %copy-done.55) | copy-start | bytes 6148
  157.3 3.9 %copy-start.64 = (f32[512]{0:T(512)S(1)}, f32[512]{0:T(512)}, u32[]{:S(2)}) copy-start(f32[512]{0:T(512)} %copy-done.63) | copy-start | bytes 6148
  157.3 52.2 %all-to-all-start.2 = ((bf16[8,8,32,512]{3,1,2,0:T(8,128)(2,1)}), bf16[8,8,32,512]{3,1,2,0:T(8,128)(2,1)S(1)}, u32[]{:S(2)}, u32[]{:S(2)}) async-start(bf16[8,8,32,512]{3,1,2,0:T(8,128)(2,1)} %bitcast.83), calls=%async_computation.3 | async-start | bytes 4194304 | tf_op jit(solution)/shard_map/all_to_all | solution.py:200
  161.2 1.9 copy-start.34
  161.2 1.9 copy-start.54
  161.2 2.2 copy-start.77
  164.9 2.9 %copy-start.48 = (f32[512]{0:T(512)S(1)}, f32[512]{0:T(512)}, u32[]{:S(2)}) copy-start(f32[512]{0:T(512)} %copy-done.47) | copy-start | bytes 6148
  164.9 2.9 %copy-start.68 = (f32[512]{0:T(512)S(1)}, f32[512]{0:T(512)}, u32[]{:S(2)}) copy-start(f32[512]{0:T(512)} %copy-done.67) | copy-start | bytes 6148
  167.8 3.3 %copy-start.7 = (f32[1024,512]{1,0:T(8,128)S(1)}, f32[1024,512]{1,0:T(8,128)}, u32[]{:S(2)}) copy-start(f32[1024,512]{1,0:T(8,128)} %get-tuple-element.51) | copy-start | bytes 6291460
  167.8 3.3 %copy-start.46 = (f32[512]{0:T(512)S(1)}, f32[512]{0:T(512)}, u32[]{:S(2)}) copy-start(f32[512]{0:T(512)} %copy-done.45) | copy-start | bytes 6148
  167.8 3.3 %copy-start.66 = (f32[512]{0:T(512)S(1)}, f32[512]{0:T(512)}, u32[]{:S(2)}) copy-start(f32[512]{0:T(512)} %copy-done.65) | copy-start | bytes 6148
  167.9 3.3 %copy-start.78 = (f32[512,512]{0,1:T(8,128)S(1)}, f32[512,512]{0,1:T(8,128)}, u32[]{:S(2)}) copy-start(f32[512,512]{0,1:T(8,128)} %copy-done.75) | copy-start | bytes 3145732
  176.7 4.6 %copy-start.85 = (f32[512]{0:T(512)S(1)}, f32[512]{0:T(512)}, u32[]{:S(2)}) copy-start(f32[512]{0:T(512)} %get-tuple-element.24) | copy-start | bytes 6148
  181.3 3.2 %copy-start.35 = (f32[512,512]{0,1:T(8,128)S(1)}, f32[512,512]{0,1:T(8,128)}, u32[]{:S(2)}) copy-start(f32[512,512]{0,1:T(8,128)} %get-tuple-element.45) | copy-start | bytes 3145732
  181.3 3.2 %copy-start.84 = (f32[512]{0:T(512)S(1)}, f32[512]{0:T(512)}, u32[]{:S(2)}) copy-start(f32[512]{0:T(512)} %get-tuple-element.25) | copy-start | bytes 6148
  184.6 2.3 copy-start.20
  209.5 5.9 %copy-start.83 = (f32[512]{0:T(512)S(1)}, f32[512]{0:T(512)}, u32[]{:S(2)}) copy-start(f32[512]{0:T(512)} %get-tuple-element.27) | copy-start | bytes 6148
  209.5 52.3 %all-to-all-start.3 = ((bf16[8,8,32,512]{3,1,2,0:T(8,128)(2,1)}), bf16[8,8,32,512]{3,1,2,0:T(8,128)(2,1)}, u32[]{:S(2)}, u32[]{:S(2)}) async-start(bf16[8,8,32,512]{3,1,2,0:T(8,128)(2,1)} %bitcast.82), calls=%async_computation.4 | async-start | bytes 4194304 | tf_op jit(solution)/shard_map/all_to_all | solution.py:207
  215.4 1.9 copy-start.12
  215.4 2.2 copy-start.32
  215.4 2.2 copy-start.50
  215.4 2.2 copy-start.52
  215.4 2.2 copy-start.82
  222.7 3.2 %copy-start.14 = (bf16[512,1024]{0,1:T(8,128)(2,1)S(1)}, bf16[512,1024]{0,1:T(8,128)(2,1)}, u32[]{:S(2)}) copy-start(bf16[512,1024]{0,1:T(8,128)(2,1)} %copy-done.13) | copy-start | bytes 3145732
  222.7 3.5 %copy-start.26 = (bf16[512,512]{0,1:T(8,128)(2,1)S(1)}, bf16[512,512]{0,1:T(8,128)(2,1)}, u32[]{:S(2)}) copy-start(bf16[512,512]{0,1:T(8,128)(2,1)} %copy-done.25) | copy-start | bytes 1572868
  222.7 3.5 %copy-start.44 = (bf16[512,512]{1,0:T(8,128)(2,1)S(1)}, bf16[512,512]{1,0:T(8,128)(2,1)}, u32[]{:S(2)}) copy-start(bf16[512,512]{1,0:T(8,128)(2,1)} %param.11) | copy-start | bytes 1572868
  224.4 2.1 copy-start.19
  261.8 5.3 %copy-start.1 = (bf16[512,2048]{1,0:T(8,128)(2,1)S(1)}, bf16[512,2048]{1,0:T(8,128)(2,1)}, u32[]{:S(2)}) copy-start(bf16[512,2048]{1,0:T(8,128)(2,1)} %param.18) | copy-start | bytes 6291460
  (28 other events, 38.6 us)
Sparse Core Ops, SparseCore 0:
  22.4 23.9 all-gather.1
  152.8 43.4 reduce-scatter.1
where the time goes:
time: 276 us; the launch traced here: 274 us
  waiting for transfers between devices  109 us (39%)
  matrix products  82.7 us (30%)
  local copies, waits for them, and re-layouts  30.8 us (11%)
  starting transfers between devices  20.2 us (7%)
  between operations  17.6 us (6%)
  other arithmetic  13.5 us (5%)
    all_to_all x1, waiting for transfers between devices, per_device(): lax.all_to_all(outgoing(memory_keys), 'mem', split_axis=0, concat_axis=0,...  38.5 us
    all_to_all x1, waiting for transfers between devices, per_device(): lax.all_to_all(send_values.reshape(mem_count, capacity, block_len, featur...  31.1 us
    dot_general x17, matrix products, contract_last(): lax.dot_general(left, right, (((1,), (1,)), ((), ())), preferred_element_...  28.6 us
    dot_general x20, matrix products, contract_first(): lax.dot_general(left, right, (((0,), (0,)), ((), ())), preferred_element_...  24.6 us
    all_to_all x1, waiting for transfers between devices, per_device(): lax.all_to_all(send_keys.reshape(mem_count, capacity, block_len, feature_...  20.5 us
    unnamed x180, local copies, waits for them, and re-layouts  20.2 us
    all_to_all x1, waiting for transfers between devices, per_device(): lax.all_to_all(outgoing(memory_values), 'mem', split_axis=0, concat_axis=...  18.4 us
    dot_general x8, matrix products, branch_forward(): jnp.dot(weights.astype(jnp.bfloat16), valueset, preferred_element_type=jn...  10.8 us
  transfers between devices with their start and end apart: 6, of which 4 were waited for; matrix products, arithmetic and copies ran while one was open for 30% of the time, Pallas kernels for 0%

commit v1 on v0

--- a/solution.py
+++ b/solution.py
@@ -5,6 +5,22 @@
 
 QBLK = 512
 keep_scale = 1.0 / 0.9
+
+
+def swapped_with_each(value, axis, split, join):
+    ways, here = (lax.axis_size(axis), lax.axis_index(axis))
+    width = value.shape[split] // ways
+    shape = list(value.shape)
+    shape[split] = width
+    height = shape[join]
+    shape[join] = height * ways
+    full = jnp.zeros(shape, value.dtype)
+    for mask in range(ways):
+        part = lax.dynamic_slice_in_dim(value, (here ^ mask) * width, width, axis=split)
+        if mask:
+            part = lax.ppermute(part, axis, [(d, d ^ mask) for d in range(ways)])
+        full = lax.dynamic_update_slice_in_dim(full, part, (here ^ mask) * height, axis=join)
+    return full
 
 
 def contract_last(left, right):
@@ -108,7 +124,7 @@
 
     fetched = (
         lax.all_to_all(outgoing(memory_keys), "mem", split_axis=0, concat_axis=0, tiled=True),
-        lax.all_to_all(outgoing(memory_values), "mem", split_axis=0, concat_axis=0, tiled=True),
+        swapped_with_each(outgoing(memory_values), "mem", 0, 0),
     )
     gate_values = 1.0 / (1.0 + jnp.exp(-gate_logit))
     keep_mask = dropout_keep.astype(jnp.float32)

time: 276 us -> 282 us (1.022)
  starting transfers between devices: 20.2 us -> 33.2 us
  matrix products: 82.7 us -> 72.3 us
  local copies, waits for them, and re-layouts: 30.8 us -> 39.6 us
  other arithmetic: 13.5 us -> 9.66 us
    ppermute x0 -> x7, waiting for transfers between devices: none -> 56.5 us  [swapped_with_each(): part = lax.ppermute(part, axis, [(d, d ^ mask) for d in range(ways)])]
    all_to_all x1, waiting for transfers between devices: 38.5 us -> 0.01 us  [per_device(): lax.all_to_all(outgoing(memory_keys), 'mem', split_axis=0, concat_axis=0,...]
    all_to_all x1 -> x0, waiting for transfers between devices: 18.4 us -> none  [per_device(): lax.all_to_all(outgoing(memory_values), 'mem', split_axis=0, concat_axis=...]
    ppermute x0 -> x7, starting transfers between devices: none -> 17.2 us  [swapped_with_each(): part = lax.ppermute(part, axis, [(d, d ^ mask) for d in range(ways)])]
    dynamic_update_slice x0 -> x7, local copies, waits for them, and re-layouts: none -> 9.88 us  [swapped_with_each(): lax.dynamic_update_slice_in_dim(full, part, (here ^ mask) * height, axis=...]
    dot_general x17, matrix products: 28.6 us -> 19.8 us  [contract_last(): lax.dot_general(left, right, (((1,), (1,)), ((), ())), preferred_element_...]
    all_to_all x1 -> x0, starting transfers between devices: 4.34 us -> none  [per_device(): lax.all_to_all(outgoing(memory_values), 'mem', split_axis=0, concat_axis=...]
    reduce_sum x8, other arithmetic: 6.68 us -> 2.98 us  [branch_forward(): row_total = jnp.sum(weights, axis=1, keepdims=True)]
  transfers between devices with their start and end apart: 6 -> 12, of which waited for: 4 -> 6; matrix products, arithmetic and copies ran while one was open for 30% -> 29% of each run, Pallas kernels for 0% -> 0%
where the time goes in v1:
time: 282 us; the launch traced here: 281 us
  waiting for transfers between devices  108 us (38%)
  matrix products  72.3 us (26%)
  local copies, waits for them, and re-layouts  39.6 us (14%)
  starting transfers between devices  33.2 us (12%)
  between operations  17.9 us (6%)
  other arithmetic  9.66 us (3%)
    ppermute x7, waiting for transfers between devices, swapped_with_each(): part = lax.ppermute(part, axis, [(d, d ^ mask) for d in range(ways)])  56.5 us
    all_to_all x1, waiting for transfers between devices, per_device(): lax.all_to_all(send_values.reshape(mem_count, capacity, block_len, featur...  31 us
    dot_general x20, matrix products, contract_first(): lax.dot_general(left, right, (((0,), (0,)), ((), ())), preferred_element_...  25 us
    dot_general x17, matrix products, contract_last(): lax.dot_general(left, right, (((1,), (1,)), ((), ())), preferred_element_...  19.8 us
    all_to_all x1, waiting for transfers between devices, per_device(): lax.all_to_all(send_keys.reshape(mem_count, capacity, block_len, feature_...  19.7 us
    unnamed x194, local copies, waits for them, and re-layouts  18.9 us
    ppermute x7, starting transfers between devices, swapped_with_each(): part = lax.ppermute(part, axis, [(d, d ^ mask) for d in range(ways)])  17.2 us
    dynamic_update_slice x7, local copies, waits for them, and re-layouts, swapped_with_each(): lax.dynamic_update_slice_in_dim(full, part, (here ^ mask) * height, axis=...  9.88 us
  transfers between devices with their start and end apart: 12, of which 6 were waited for; matrix products, arithmetic and copies ran while one was open for 29% of the time, Pallas kernels for 0%

profile of v1, /device:TPU:0, one launch (start us, length us, event | category | flops | bytes accessed | tf_op | source)
XLA Modules:
  0.0 280.6 jit_solution(1370060497834902825)
XLA Ops:
  9.8 1.3 copy.64
  11.1 2.1 convolution_convert_fusion.3
  13.2 7.4 %all-to-all-start = ((bf16[8,8,32,512]{3,1,2,0:T(8,128)(2,1)}), bf16[8,8,32,512]{3,1,2,0:T(8,128)(2,1)}, u32[]{:S(2)}, u32[]{:S(2)}) async-start(bf16[8,8,32,512]{3,1,2,0:T(8,128)(2,1)} %bitcast.82), calls=%async_computation | async-start | bytes 4194304 | tf_op jit(solution)/shard_map/all_to_all | solution.py:126
  21.0 2.1 convolution_convert_fusion.2
  23.3 1.4 copy-done.2
  24.7 1.2 constant_dynamic-slice_fusion.6
  25.9 4.6 %collective-permute-start.6 = (bf16[1,8,32,512]{3,1,2,0:T(8,128)(2,1)S(1)}, bf16[1,8,32,512]{3,1,2,0:T(8,128)(2,1)}, u32[]{:S(2)}, u32[]{:S(2)}) collective-permute-start(bf16[1,8,32,512]{3,1,2,0:T(8,128)(2,1)S(1)} %get-tuple-element.34), channel_id=1, source_target_pairs={{0,28},{4,24},{8,20},{12,16},{16,12},{20,8},{24,4},{28,0},{1,29},{... | collective-permute-start | bytes 786440 | tf_op jit(solution)/shard_map/ppermute | solution.py:21
  31.1 1.5 collective-permute-start.1
  32.7 1.9 collective-permute-start
  37.1 1.1 convolution_divide_fusion.2
  44.3 1.3 copy.42
  45.7 1.7 collective-permute-start.3
  47.5 1.7 constant_dynamic-update-slice_fusion.5
  49.1 30.2 %collective-permute-done.1 = bf16[1,8,32,512]{3,1,2,0:T(8,128)(2,1)} collective-permute-done((bf16[1,8,32,512]{3,1,2,0:T(8,128)(2,1)}, bf16[1,8,32,512]{3,1,2,0:T(8,128)(2,1)}, u32[]{:S(2)}, u32[]{:S(2)}) %collective-permute-start.1) | collective-permute-done | bytes 262176 | tf_op jit(solution)/shard_map/ppermute | solution.py:21
  79.3 6.8 %collective-permute-start.4 = (bf16[1,8,32,512]{3,1,2,0:T(8,128)(2,1)}, bf16[1,8,32,512]{3,1,2,0:T(8,128)(2,1)S(1)}, u32[]{:S(2)}, u32[]{:S(2)}) collective-permute-start(bf16[1,8,32,512]{3,1,2,0:T(8,128)(2,1)} %get-tuple-element.36), channel_id=1, source_target_pairs={{0,20},{4,16},{8,28},{12,24},{16,4},{20,0},{24,12},{28,8},{1,21},{... | collective-permute-start | bytes 786440 | tf_op jit(solution)/shard_map/ppermute | solution.py:21
  86.1 1.6 constant_dynamic-update-slice_fusion.4
  87.8 1.7 constant_dynamic-update-slice_fusion.3
  89.4 20.1 %collective-permute-done.3 = bf16[1,8,32,512]{3,1,2,0:T(8,128)(2,1)S(1)} collective-permute-done((bf16[1,8,32,512]{3,1,2,0:T(8,128)(2,1)}, bf16[1,8,32,512]{3,1,2,0:T(8,128)(2,1)S(1)}, u32[]{:S(2)}, u32[]{:S(2)}) %collective-permute-start.3) | collective-permute-done | bytes 262176 | tf_op jit(solution)/shard_map/ppermute | solution.py:21
  110.3 6.1 %collective-permute-done.4 = bf16[1,8,32,512]{3,1,2,0:T(8,128)(2,1)S(1)} collective-permute-done((bf16[1,8,32,512]{3,1,2,0:T(8,128)(2,1)}, bf16[1,8,32,512]{3,1,2,0:T(8,128)(2,1)S(1)}, u32[]{:S(2)}, u32[]{:S(2)}) %collective-permute-start.4) | collective-permute-done | bytes 262176 | tf_op jit(solution)/shard_map/ppermute | solution.py:21
  117.1 1.7 constant_dynamic-update-slice_fusion
  118.8 1.7 constant_dynamic-update-slice_fusion.6
  120.5 2.1 convolution_convert_fusion.4
  122.6 1.3 reshape.130
  123.9 3.2 %fusion.8 = f32[512,512]{0,1:T(8,128)S(1)} fusion(bf16[512,2048]{1,0:T(8,128)(2,1)} %all-gather.2.cloned.1.call-done, bf16[512,2048]{1,0:T(8,128)(2,1)S(1)} %copy-done, s32[512,512]{0,1:T(8,128)} %copy.42), kind=kOutput, calls=%fused_computation.37 | convolution fusion | flops 1074528256 | bytes 6291456 | tf_op jit(solution)/shard_map/dot_general | solution.py:27
  128.5 3.1 %convolution_convert_fusion.5 = bf16[32,16384]{1,0:T(8,128)(2,1)} fusion(bf16[64,16384]{1,0:T(8,128)(2,1)} %bitcast.3, s32[32]{0:T(128)S(1)} %fusion.184), kind=kOutput, calls=%fused_computation.5 | convolution fusion | flops 67635200 | bytes 3145856 | tf_op jit(solution)/shard_map/dot_general | solution.py:122
  131.6 1.7 reshape.126
  133.4 1.4 multiply_reduce_fusion
  136.6 1.1 copy-done.40
  140.4 3.3 %multiply_reduce_fusion.10 = (f32[512]{0:T(512)}, f32[512]{0:T(512)}, f32[512]{0:T(512)S(1)}, f32[512]{0:T(512)}, f32[512]{0:T(512)S(1)}, /*index=5*/f32[512]{0:...) fusion(f32[512,512]{0,1:T(8,128)S(1)} %copy-done.83, f32[]{:T(128)S(6)} %sub.91, ...), kind=kOutput, calls=%fused_computation.152 | convolution fusion | flops 69268480 | bytes 4342800 | tf_op jit(solution)/shard_map/dot_general | solution.py:52
  143.7 1.3 fusion.3
  145.1 1.4 fusion.1
  147.0 1.2 convolution_convert_fusion.13
  149.5 1.8 multiply_reduce_fusion.11
  151.4 1.3 fusion.5
  152.7 1.4 fusion.7
  154.1 1.2 convolution_convert_fusion.15
  155.3 1.2 convolution_convert_fusion.14
  156.4 3.3 %fusion.71 = f32[512,2048]{1,0:T(8,128)} fusion(bf16[512,2048]{1,0:T(8,128)(2,1)S(1)} %copy-done, f32[512,128]{0,1:T(8,128)S(1)} %get-tuple-element.43, f32[512,128]{0,1:T(8,128)S(1)} %get-tuple-element.42, f32[512,128]{0,1:T(8,128)S(1)} %get-tuple-element.44, f32[512,128]{0,1:T(8,128)S(1)} %get-tuple-element.45, s32[512,512]{0,1:T(8,128)S(1)} %copy-done.22), kind=kOutput, calls=%fused_computation.132 | convolution fusion | flops 1075576832 | bytes 8388608 | tf_op jit(solution)/shard_map/dot_general | solution.py:160
  162.0 2.2 convolution_convert_fusion.1
  164.3 4.0 %all-to-all-start.1 = ((bf16[8,8,32,512]{3,1,2,0:T(8,128)(2,1)}), bf16[8,8,32,512]{3,1,2,0:T(8,128)(2,1)S(1)}, u32[]{:S(2)}, u32[]{:S(2)}) async-start(bf16[8,8,32,512]{3,1,2,0:T(8,128)(2,1)} %bitcast.85), calls=%async_computation.2 | async-start | bytes 4194304 | tf_op jit(solution)/shard_map/all_to_all | solution.py:216
  168.3 1.8 convolution_convert_fusion.19
  172.8 2.0 copy.55
  174.9 3.5 %convolution_convert_fusion.8 = bf16[1024,128]{0,1:T(8,128)(2,1)S(1)} fusion(f32[1024,512]{1,0:T(8,128)} %copy-done.9, f32[512]{0:T(512)} %copy-done.75, f32[512]{0:T(512)} %copy-done.49, f32[512,512]{0,1:T(8,128)} %copy-done.82, f32[]{:T(128)} %bitcast.8), kind=kOutput, calls=%fused_computation.70 | convolution fusion | flops 136577024 | bytes 2626048 | tf_op jit(solution)/shard_map/dot_general | solution.py:33
  178.5 1.4 convolution_convert_fusion.9
  180.1 1.4 convolution_convert_fusion.10
  181.6 1.3 convolution_convert_fusion.11
  182.9 1.1 pad_maximum_fusion.1
  184.0 2.3 copy.52
  186.3 2.3 reshape.135
  188.7 1.8 fusion.36
  190.5 1.4 convolution_convert_fusion.23
  192.0 2.2 fusion.33
  194.2 2.2 convolution_convert_fusion
  196.5 19.7 %all-to-all-done.1 = bf16[8,8,32,512]{3,1,2,0:T(8,128)(2,1)S(1)} async-done(((bf16[8,8,32,512]{3,1,2,0:T(8,128)(2,1)}), bf16[8,8,32,512]{3,1,2,0:T(8,128)(2,1)S(1)}, u32[]{:S(2)}, u32[]{:S(2)}) %all-to-all-start.1) | async-done | bytes 2097184 | tf_op jit(solution)/shard_map/all_to_all | solution.py:216
  216.2 4.5 %all-to-all-start.2 = ((bf16[8,8,32,512]{3,1,2,0:T(8,128)(2,1)}), bf16[8,8,32,512]{3,1,2,0:T(8,128)(2,1)}, u32[]{:S(2)}, u32[]{:S(2)}) async-start(bf16[8,8,32,512]{3,1,2,0:T(8,128)(2,1)} %bitcast.84), calls=%async_computation.3 | async-start | bytes 4194304 | tf_op jit(solution)/shard_map/all_to_all | solution.py:223
  220.7 1.4 convolution_convert_fusion.20
  222.2 1.8 fusion.34
  224.4 1.4 fusion.35
  227.4 2.0 copy.54
  229.5 1.7 fusion.100
  231.2 1.4 fusion.40
  237.4 31.0 %all-to-all-done.2 = bf16[8,8,32,512]{3,1,2,0:T(8,128)(2,1)} async-done(((bf16[8,8,32,512]{3,1,2,0:T(8,128)(2,1)}), bf16[8,8,32,512]{3,1,2,0:T(8,128)(2,1)}, u32[]{:S(2)}, u32[]{:S(2)}) %all-to-all-start.2) | async-done | bytes 2097184 | tf_op jit(solution)/shard_map/all_to_all | solution.py:223
  268.5 2.2 convolution_convert_fusion.6
  271.7 2.1 convert_element_type.216
  (253 shorter events, 31.7 us)
Async XLA Ops:
  7.2 116.8 %copy-start = (bf16[512,2048]{1,0:T(8,128)(2,1)S(1)}, bf16[512,2048]{1,0:T(8,128)(2,1)}, u32[]{:S(2)}) copy-start(bf16[512,2048]{1,0:T(8,128)(2,1)} %param.18) | copy-start | bytes 6291460
  7.2 116.8 %all-gather.2.cloned.1.call-start = ((), (), s32[]{:S(2)}) async-start(), calls=%async_computation.5 | async-start | bytes 2621440 | tf_op jit(solution)/shard_map/all_gather | solution.py:164
  13.2 7.5 %copy-start.44 = (bf16[16,32,512]{2,1,0:T(8,128)(2,1)S(1)}, bf16[16,32,512]{2,1,0:T(8,128)(2,1)}, u32[]{:S(2)}) copy-start(bf16[16,32,512]{2,1,0:T(8,128)(2,1)} %param.14) | copy-start | bytes 1572868
  13.2 115.4 %all-to-all-start = ((bf16[8,8,32,512]{3,1,2,0:T(8,128)(2,1)}), bf16[8,8,32,512]{3,1,2,0:T(8,128)(2,1)}, u32[]{:S(2)}, u32[]{:S(2)}) async-start(bf16[8,8,32,512]{3,1,2,0:T(8,128)(2,1)} %bitcast.82), calls=%async_computation | async-start | bytes 4194304 | tf_op jit(solution)/shard_map/all_to_all | solution.py:126
  20.6 251.1 %reduce-scatter.2.cloned.1.call-start = ((), (), s32[]{:S(2)}) async-start(), calls=%async_computation.4 | async-start | bytes 5242880 | tf_op jit(solution)/shard_map/reduce_scatter | solution.py:161
  24.7 9.9 %copy-start.11 = (bf16[512,512]{1,0:T(8,128)(2,1)S(1)}, bf16[512,512]{1,0:T(8,128)(2,1)}, u32[]{:S(2)}) copy-start(bf16[512,512]{1,0:T(8,128)(2,1)} %param.10) | copy-start | bytes 1572868
  24.7 9.9 %copy-start.45 = (bf16[512,512]{1,0:T(8,128)(2,1)S(1)}, bf16[512,512]{1,0:T(8,128)(2,1)}, u32[]{:S(2)}) copy-start(bf16[512,512]{1,0:T(8,128)(2,1)} %param.11) | copy-start | bytes 1572868
  25.9 9.7 %copy-start.10 = (bf16[8,8,32,512]{3,1,2,0:T(8,128)(2,1)}, bf16[8,8,32,512]{3,1,2,0:T(8,128)(2,1)S(1)}, u32[]{:S(2)}) copy-start(bf16[8,8,32,512]{3,1,2,0:T(8,128)(2,1)S(1)} %get-tuple-element.41) | copy-start | bytes 6291460
  25.9 92.9 %collective-permute-start.6 = (bf16[1,8,32,512]{3,1,2,0:T(8,128)(2,1)S(1)}, bf16[1,8,32,512]{3,1,2,0:T(8,128)(2,1)}, u32[]{:S(2)}, u32[]{:S(2)}) collective-permute-start(bf16[1,8,32,512]{3,1,2,0:T(8,128)(2,1)S(1)} %get-tuple-element.34), channel_id=1, source_target_pairs={{0,28},{4,24},{8,20},{12,16},{16,12},{20,8},{24,4},{28,0},{1,29},{... | collective-permute-start | bytes 786440 | tf_op jit(solution)/shard_map/ppermute | solution.py:21
  30.5 86.6 %collective-permute-start.5 = (bf16[1,8,32,512]{3,1,2,0:T(8,128)(2,1)}, bf16[1,8,32,512]{3,1,2,0:T(8,128)(2,1)}, u32[]{:S(2)}, u32[]{:S(2)}) collective-permute-start(bf16[1,8,32,512]{3,1,2,0:T(8,128)(2,1)} %get-tuple-element.35), channel_id=1, source_target_pairs={{0,24},{4,28},{8,16},{12,20},{16,8},{20,12},{24,0},{28,4},{1,25},{... | collective-permute-start | bytes 786440 | tf_op jit(solution)/shard_map/ppermute | solution.py:21
  31.1 56.6 %collective-permute-start.2 = (bf16[1,8,32,512]{3,1,2,0:T(8,128)(2,1)}, bf16[1,8,32,512]{3,1,2,0:T(8,128)(2,1)}, u32[]{:S(2)}, u32[]{:S(2)}) collective-permute-start(bf16[1,8,32,512]{3,1,2,0:T(8,128)(2,1)} %get-tuple-element.38), channel_id=1, source_target_pairs={{0,12},{4,8},{8,4},{12,0},{16,28},{20,24},{24,20},{28,16},{1,13},{... | collective-permute-start | bytes 786440 | tf_op jit(solution)/shard_map/ppermute | solution.py:21
  31.1 48.2 %collective-permute-start.1 = (bf16[1,8,32,512]{3,1,2,0:T(8,128)(2,1)}, bf16[1,8,32,512]{3,1,2,0:T(8,128)(2,1)}, u32[]{:S(2)}, u32[]{:S(2)}) collective-permute-start(bf16[1,8,32,512]{3,1,2,0:T(8,128)(2,1)} %get-tuple-element.39), channel_id=1, source_target_pairs={{0,8},{4,12},{8,0},{12,4},{16,24},{20,28},{24,16},{28,20},{1,9},{5... | collective-permute-start | bytes 786440 | tf_op jit(solution)/shard_map/ppermute | solution.py:21
  32.7 13.1 %collective-permute-start = (bf16[1,8,32,512]{3,1,2,0:T(8,128)(2,1)}, bf16[1,8,32,512]{3,1,2,0:T(8,128)(2,1)}, u32[]{:S(2)}, u32[]{:S(2)}) collective-permute-start(bf16[1,8,32,512]{3,1,2,0:T(8,128)(2,1)} %get-tuple-element.40), channel_id=1, source_target_pairs={{0,4},{4,0},{8,12},{12,8},{16,20},{20,16},{24,28},{28,24},{1,5},{5... | collective-permute-start | bytes 786440 | tf_op jit(solution)/shard_map/ppermute | solution.py:21
  34.9 92.2 %copy-start.50 = (f32[512]{0:T(512)}, f32[512]{0:T(512)S(1)}, u32[]{:S(2)}) copy-start(f32[512]{0:T(512)S(1)} %get-tuple-element.60) | copy-start | bytes 6148
  35.3 2.9 %copy-start.35 = (f32[512,512]{0,1:T(8,128)}, f32[512,512]{0,1:T(8,128)S(1)}, u32[]{:S(2)}) copy-start(f32[512,512]{0,1:T(8,128)S(1)} %get-tuple-element.53) | copy-start | bytes 3145732
  35.3 2.9 %copy-start.60 = (f32[512]{0:T(512)}, f32[512]{0:T(512)S(1)}, u32[]{:S(2)}) copy-start(f32[512]{0:T(512)S(1)} %get-tuple-element.52) | copy-start | bytes 6148
  35.6 3.6 %copy-start.33 = (f32[512,512]{0,1:T(8,128)}, f32[512,512]{0,1:T(8,128)S(1)}, u32[]{:S(2)}) copy-start(f32[512,512]{0,1:T(8,128)S(1)} %get-tuple-element.57) | copy-start | bytes 3145732
  35.6 3.6 %copy-start.54 = (f32[512]{0:T(512)}, f32[512]{0:T(512)S(1)}, u32[]{:S(2)}) copy-start(f32[512]{0:T(512)S(1)} %get-tuple-element.56) | copy-start | bytes 6148
  35.9 91.3 %copy-start.52 = (f32[512]{0:T(512)}, f32[512]{0:T(512)S(1)}, u32[]{:S(2)}) copy-start(f32[512]{0:T(512)S(1)} %fusion.59) | copy-start | bytes 6148
  36.3 2.9 %copy-start.57 = (f32[512]{0:T(512)}, f32[512]{0:T(512)S(1)}, u32[]{:S(2)}) copy-start(f32[512]{0:T(512)S(1)} %fusion.62) | copy-start | bytes 6148
  37.1 3.2 %copy-start.38 = (f32[512,512]{0,1:T(8,128)}, f32[512,512]{0,1:T(8,128)S(1)}, u32[]{:S(2)}) copy-start(f32[512,512]{0,1:T(8,128)S(1)} %get-tuple-element.51) | copy-start | bytes 3145732
  37.1 3.2 %copy-start.66 = (f32[512]{0:T(512)}, f32[512]{0:T(512)S(1)}, u32[]{:S(2)}) copy-start(f32[512]{0:T(512)S(1)} %get-tuple-element.50) | copy-start | bytes 6148
  38.2 6.2 %copy-start.29 = (s32[512,512]{1,0:T(8,128)S(1)}, s32[512,512]{1,0:T(8,128)}, u32[]{:S(2)}) copy-start(s32[512,512]{1,0:T(8,128)} %param.17) | copy-start | bytes 3145732
  45.7 63.8 %collective-permute-start.3 = (bf16[1,8,32,512]{3,1,2,0:T(8,128)(2,1)}, bf16[1,8,32,512]{3,1,2,0:T(8,128)(2,1)S(1)}, u32[]{:S(2)}, u32[]{:S(2)}) collective-permute-start(bf16[1,8,32,512]{3,1,2,0:T(8,128)(2,1)} %get-tuple-element.37), channel_id=1, source_target_pairs={{0,16},{4,20},{8,24},{12,28},{16,0},{20,4},{24,8},{28,12},{1,17},{... | collective-permute-start | bytes 786440 | tf_op jit(solution)/shard_map/ppermute | solution.py:21
  79.3 37.1 %collective-permute-start.4 = (bf16[1,8,32,512]{3,1,2,0:T(8,128)(2,1)}, bf16[1,8,32,512]{3,1,2,0:T(8,128)(2,1)S(1)}, u32[]{:S(2)}, u32[]{:S(2)}) collective-permute-start(bf16[1,8,32,512]{3,1,2,0:T(8,128)(2,1)} %get-tuple-element.36), channel_id=1, source_target_pairs={{0,20},{4,16},{8,28},{12,24},{16,4},{20,0},{24,12},{28,8},{1,21},{... | collective-permute-start | bytes 786440 | tf_op jit(solution)/shard_map/ppermute | solution.py:21
  123.9 4.2 %copy-start.31 = (f32[512,512]{0,1:T(8,128)S(1)}, f32[512,512]{0,1:T(8,128)}, u32[]{:S(2)}) copy-start(f32[512,512]{0,1:T(8,128)} %copy-done.30) | copy-start | bytes 3145732
  134.8 10.3 %copy-start.9 = (f32[1024,512]{1,0:T(8,128)}, f32[1024,512]{1,0:T(8,128)S(1)}, u32[]{:S(2)}) copy-start(f32[1024,512]{1,0:T(8,128)S(1)} %get-tuple-element.55) | copy-start | bytes 6291460
  134.8 10.3 %copy-start.49 = (f32[512]{0:T(512)}, f32[512]{0:T(512)S(1)}, u32[]{:S(2)}) copy-start(f32[512]{0:T(512)S(1)} %get-tuple-element.54) | copy-start | bytes 6148
  135.2 8.5 %copy-start.7 = (f32[1024,512]{1,0:T(8,128)}, f32[1024,512]{1,0:T(8,128)S(1)}, u32[]{:S(2)}) copy-start(f32[1024,512]{1,0:T(8,128)S(1)} %get-tuple-element.59) | copy-start | bytes 6291460
  135.2 8.5 %copy-start.47 = (f32[512]{0:T(512)}, f32[512]{0:T(512)S(1)}, u32[]{:S(2)}) copy-start(f32[512]{0:T(512)S(1)} %get-tuple-element.58) | copy-start | bytes 6148
  135.7 15.6 %copy-start.5 = (f32[1024,512]{1,0:T(8,128)}, f32[1024,512]{1,0:T(8,128)S(1)}, u32[]{:S(2)}) copy-start(f32[1024,512]{1,0:T(8,128)S(1)} %get-tuple-element.66) | copy-start | bytes 6291460
  136.2 16.5 %copy-start.3 = (f32[1024,512]{1,0:T(8,128)}, f32[1024,512]{1,0:T(8,128)S(1)}, u32[]{:S(2)}) copy-start(f32[1024,512]{1,0:T(8,128)S(1)} %get-tuple-element.64) | copy-start | bytes 6291460
  137.7 7.4 %copy-start.75 = (f32[512]{0:T(512)}, f32[512]{0:T(512)S(1)}, u32[]{:S(2)}) copy-start(f32[512]{0:T(512)S(1)} %fusion.31) | copy-start | bytes 6148
  138.6 5.1 %copy-start.73 = (f32[512]{0:T(512)}, f32[512]{0:T(512)S(1)}, u32[]{:S(2)}) copy-start(f32[512]{0:T(512)S(1)} %fusion.28) | copy-start | bytes 6148
  148.6 2.8 copy-start.78
  149.5 3.2 %copy-start.76 = (f32[512]{0:T(512)}, f32[512]{0:T(512)S(1)}, u32[]{:S(2)}) copy-start(f32[512]{0:T(512)S(1)} %fusion.22) | copy-start | bytes 6148
  152.6 2.6 copy-start.19
  154.0 2.4 copy-start.17
  154.1 2.4 copy-start.22
  164.2 4.0 %copy-start.68 = (f32[512]{0:T(512)S(1)}, f32[512]{0:T(512)}, u32[]{:S(2)}) copy-start(f32[512]{0:T(512)} %copy-done.66) | copy-start | bytes 6148
  164.3 4.0 %copy-start.71 = (f32[512]{0:T(512)S(1)}, f32[512]{0:T(512)}, u32[]{:S(2)}) copy-start(f32[512]{0:T(512)} %fusion.56) | copy-start | bytes 6148
  164.3 51.9 %all-to-all-start.1 = ((bf16[8,8,32,512]{3,1,2,0:T(8,128)(2,1)}), bf16[8,8,32,512]{3,1,2,0:T(8,128)(2,1)S(1)}, u32[]{:S(2)}, u32[]{:S(2)}) async-start(bf16[8,8,32,512]{3,1,2,0:T(8,128)(2,1)} %bitcast.85), calls=%async_computation.2 | async-start | bytes 4194304 | tf_op jit(solution)/shard_map/all_to_all | solution.py:216
  174.9 3.5 %copy-start.8 = (f32[1024,512]{1,0:T(8,128)S(1)}, f32[1024,512]{1,0:T(8,128)}, u32[]{:S(2)}) copy-start(f32[1024,512]{1,0:T(8,128)} %copy-done.7) | copy-start | bytes 6291460
  174.9 3.5 %copy-start.48 = (f32[512]{0:T(512)S(1)}, f32[512]{0:T(512)}, u32[]{:S(2)}) copy-start(f32[512]{0:T(512)} %copy-done.47) | copy-start | bytes 6148
  174.9 3.5 %copy-start.74 = (f32[512]{0:T(512)S(1)}, f32[512]{0:T(512)}, u32[]{:S(2)}) copy-start(f32[512]{0:T(512)} %copy-done.73) | copy-start | bytes 6148
  174.9 3.5 %copy-start.85 = (f32[512,512]{0,1:T(8,128)S(1)}, f32[512,512]{0,1:T(8,128)}, u32[]{:S(2)}) copy-start(f32[512,512]{0,1:T(8,128)} %copy-done.82) | copy-start | bytes 3145732
  184.0 4.7 %copy-start.69 = (f32[512]{0:T(512)S(1)}, f32[512]{0:T(512)}, u32[]{:S(2)}) copy-start(f32[512]{0:T(512)} %copy-done.66) | copy-start | bytes 6148
  184.0 4.7 %copy-start.72 = (f32[512]{0:T(512)S(1)}, f32[512]{0:T(512)}, u32[]{:S(2)}) copy-start(f32[512]{0:T(512)} %fusion.56) | copy-start | bytes 6148
  184.0 4.7 %copy-start.92 = (f32[512]{0:T(512)S(1)}, f32[512]{0:T(512)}, u32[]{:S(2)}) copy-start(f32[512]{0:T(512)} %get-tuple-element.24) | copy-start | bytes 6148
  188.7 3.3 %copy-start.37 = (f32[512,512]{0,1:T(8,128)S(1)}, f32[512,512]{0,1:T(8,128)}, u32[]{:S(2)}) copy-start(f32[512,512]{0,1:T(8,128)} %copy-done.35) | copy-start | bytes 3145732
  188.7 3.3 %copy-start.62 = (f32[512]{0:T(512)S(1)}, f32[512]{0:T(512)}, u32[]{:S(2)}) copy-start(f32[512]{0:T(512)} %copy-done.60) | copy-start | bytes 6148
  188.7 3.3 %copy-start.65 = (f32[512]{0:T(512)S(1)}, f32[512]{0:T(512)}, u32[]{:S(2)}) copy-start(f32[512]{0:T(512)} %copy-done.63) | copy-start | bytes 6148
  188.7 3.3 %copy-start.91 = (f32[512]{0:T(512)S(1)}, f32[512]{0:T(512)}, u32[]{:S(2)}) copy-start(f32[512]{0:T(512)} %get-tuple-element.25) | copy-start | bytes 6148
  192.0 2.3 copy-start.21
  216.2 5.9 %copy-start.56 = (f32[512]{0:T(512)S(1)}, f32[512]{0:T(512)}, u32[]{:S(2)}) copy-start(f32[512]{0:T(512)} %copy-done.54) | copy-start | bytes 6148
  216.2 5.9 %copy-start.59 = (f32[512]{0:T(512)S(1)}, f32[512]{0:T(512)}, u32[]{:S(2)}) copy-start(f32[512]{0:T(512)} %copy-done.57) | copy-start | bytes 6148
  216.2 5.9 %copy-start.90 = (f32[512]{0:T(512)S(1)}, f32[512]{0:T(512)}, u32[]{:S(2)}) copy-start(f32[512]{0:T(512)} %get-tuple-element.27) | copy-start | bytes 6148
  216.2 52.3 %all-to-all-start.2 = ((bf16[8,8,32,512]{3,1,2,0:T(8,128)(2,1)}), bf16[8,8,32,512]{3,1,2,0:T(8,128)(2,1)}, u32[]{:S(2)}, u32[]{:S(2)}) async-start(bf16[8,8,32,512]{3,1,2,0:T(8,128)(2,1)} %bitcast.84), calls=%async_computation.3 | async-start | bytes 4194304 | tf_op jit(solution)/shard_map/all_to_all | solution.py:223
  222.1 2.2 copy-start.32
  222.1 2.2 copy-start.51
  229.5 3.2 %copy-start.15 = (bf16[512,1024]{0,1:T(8,128)(2,1)S(1)}, bf16[512,1024]{0,1:T(8,128)(2,1)}, u32[]{:S(2)}) copy-start(bf16[512,1024]{0,1:T(8,128)(2,1)} %copy-done.14) | copy-start | bytes 3145732
  229.5 3.5 %copy-start.26 = (bf16[512,512]{0,1:T(8,128)(2,1)S(1)}, bf16[512,512]{0,1:T(8,128)(2,1)}, u32[]{:S(2)}) copy-start(bf16[512,512]{0,1:T(8,128)(2,1)} %copy-done.25) | copy-start | bytes 1572868
  229.5 3.5 %copy-start.46 = (bf16[512,512]{1,0:T(8,128)(2,1)S(1)}, bf16[512,512]{1,0:T(8,128)(2,1)}, u32[]{:S(2)}) copy-start(bf16[512,512]{1,0:T(8,128)(2,1)} %param.11) | copy-start | bytes 1572868
  268.5 5.3 %copy-start.1 = (bf16[512,2048]{1,0:T(8,128)(2,1)S(1)}, bf16[512,2048]{1,0:T(8,128)(2,1)}, u32[]{:S(2)}) copy-start(bf16[512,2048]{1,0:T(8,128)(2,1)} %param.18) | copy-start | bytes 6291460
  (41 other events, 63.1 us)
Sparse Core Ops, SparseCore 0:
  9.6 25.2 all-gather.1
  159.9 43.1 reduce-scatter.1
